TPU v7x, 32 devices: a whole 2x2x4 slice. The times are simulated.
32 devices in a mesh: grp: 8 (over y, x, core), mem: 4 (over z).
Axes of the slice: x: 2, y: 2, z: 4, core: 2. Of those that a mesh axis runs over, the one named last changes fastest.
Arguments:
- points: float32 [16, 32768], P(None, ('grp', 'mem')), may hold values from -6 to 6
- residual: float32 [16, 32768], P(None, ('grp', 'mem')), may hold values from -6 to 6
- coef: float32 [16, 32768], P(None, ('grp', 'mem')), may hold values from -3 to 3
- block_of: int32 [32768], P(('grp', 'mem')), may hold values from 0 to 7, as said below
- order: int32 [2], replicated, may hold values from 0 to 7
- inverse: float32 [8, 4096, 4096], P('grp', 'mem'), may hold values from -1 to 2
Outputs:
- residual_out: float32 [16, 32768], P(None, ('grp', 'mem'))
- coef_out: float32 [16, 32768], P(None, ('grp', 'mem'))
Inputs may be any that keep to these rules, and one draw needn't show every extreme that they name: `block_of`: each run of 1024 consecutive points (the points of one device) holds exactly 128 points of every block.
All inputs are finite; a program needn't handle non-finite values.
Results may differ from a plain program's by a relative error of at most 0.00013.
Values sent between devices are 32-bit elements; how exact they have to be, the bound alone decides.
No kernel may reach another device: no remote copies, remote signals or barrier semaphores. Data moves between devices by JAX's collectives and lax.ppermute only.
A program may use at most 128 MiB of HBM per device.

v0:
```python
import jax
import jax.numpy as jnp
from jax import lax
from jax.sharding import PartitionSpec as P

B = 4096
STEPS = 2
ridge_weight = 0.5
kernel_scale = 0.125


def from_root(value, axis, source):
    kept = jnp.where(lax.axis_index(axis) == source, value, 0).astype(value.dtype)
    return lax.psum(kept, axis)


def body(points, residual, coef, block_of, order, inverse):
    highest = lax.Precision.HIGHEST
    n_mem = lax.axis_size("mem")
    per = B // (lax.axis_size("grp") * n_mem)
    slots = inverse.shape[0]
    mine = lax.axis_index("grp") * n_mem + lax.axis_index("mem")
    norms_local = jnp.sum(points * points, axis=0)
    for step_index in range(STEPS):
        block_id = order[step_index]
        inside = block_of == block_id
        position = jnp.cumsum(inside.astype(jnp.int32)) - 1
        select = (
            (position[:, None] == jnp.arange(per, dtype=jnp.int32)[None, :]) & inside[:, None]
        ).astype(jnp.float32)
        chosen_res = jnp.dot(residual, select, precision=highest)
        chosen_pts = jnp.dot(points, select, precision=highest)
        block_res, block_pts = (
            lax.all_gather(chosen_res, ("grp", "mem"), axis=1, tiled=True),
            lax.all_gather(chosen_pts, ("grp", "mem"), axis=1, tiled=True),
        )
        matrix_rows = lax.dynamic_index_in_dim(inverse, block_id % slots, 0, keepdims=False)
        solved = lax.dot_general(
            block_res, matrix_rows, (((1,), (1,)), ((), ())), precision=highest
        )
        owner = block_id // slots
        norms_block = jnp.sum(block_pts * block_pts, axis=0)
        assembled = lax.all_gather(solved, "mem", axis=1, tiled=True)
        assembled = from_root(assembled, "grp", owner)
        width = assembled.shape[1]
        cross = lax.dot_general(points, block_pts, (((0,), (0,)), ((), ())), precision=highest)
        kernel = jnp.exp(
            -kernel_scale * (norms_local[:, None] + norms_block[None, :] - 2.0 * cross)
        )
        total_update = lax.dot_general(
            assembled, kernel, (((1,), (1,)), ((), ())), precision=highest
        )
        ranks = jnp.arange(width, dtype=jnp.int32)
        wanted = mine * per + jnp.arange(per, dtype=jnp.int32)
        picker = (ranks[:, None] == wanted[None, :]).astype(jnp.float32)
        owned = jnp.dot(assembled, picker, precision=highest)
        update, owned = (total_update, owned)
        spread_back = lax.dot_general(owned, select, (((1,), (1,)), ((), ())), precision=highest)
        residual = residual - update - ridge_weight * spread_back
        coef = coef + spread_back
    return (residual, coef)


def solution(mesh):
    in_specs = (
        P(None, ("grp", "mem")),
        P(None, ("grp", "mem")),
        P(None, ("grp", "mem")),
        P(("grp", "mem")),
        P(),
        P("grp", "mem", None),
    )
    out_specs = (P(None, ("grp", "mem")), P(None, ("grp", "mem")))
    return jax.shard_map(body, mesh=mesh, in_specs=in_specs, out_specs=out_specs, check_vma=False)
```

profile of v0, /device:TPU:0, one launch (start us, length us, event | category | flops | bytes accessed | tf_op | source)
XLA Modules:
  0.0 461.2 jit_solution(17110810315561444372)
XLA Ops:
  7.2 0.0 copy-start
  7.2 0.0 all-reduce.3.cloned.1.call-start
  7.2 1.3 fusion.67
  8.5 2.0 convert_bitcast_fusion
  10.5 0.3 reduce-window.16
  10.8 0.1 slice.21
  10.9 0.1 slice_reduce_fusion.1
  11.0 0.1 add_bitcast_fusion.1
  11.1 1.4 convolution_bitcast_fusion.2
  12.5 71.8 %all_gather.18 = f32[16,4096]{1,0:T(8,128)S(1)} all-gather(f32[16,128]{1,0:T(8,128)S(1)} %convolution_bitcast_fusion.2), channel_id=1, replica_groups=mesh['grp'=8,'mem'=4] {'grp','mem'}, dimensions={1}, use_global_device_ids=true | all-gather | bytes 270336 | tf_op jit(solution)/shard_map/all_gather | solution.py:34
  84.3 17.1 %fusion.10 = f32[16,1024]{1,0:T(8,128)S(1)} fusion(f32[16,4096]{1,0:T(8,128)S(1)} %all_gather.18, f32[1,1024,4096]{2,1,0:T(8,128)} %param.11), kind=kOutput, calls=%fused_computation.10 | convolution fusion | flops 805306368 | bytes 17104896 | tf_op jit(solution)/shard_map/dot_general | solution.py:38
  101.4 0.0 copy-start.1
  101.4 14.3 %all_gather.19 = f32[16,4096]{1,0:T(8,128)S(1)} all-gather(f32[16,1024]{1,0:T(8,128)S(1)} %fusion.10), channel_id=1, replica_groups=mesh['grp'=8,'mem'=4] {'mem'}, dimensions={1}, use_global_device_ids=true | all-gather | bytes 327680 | tf_op jit(solution)/shard_map/all_gather | solution.py:43
  116.4 0.7 broadcast_select_fusion.1
  117.1 0.0 all-reduce.3.cloned.1.call-update
  117.1 0.0 all-reduce.5.cloned.1.call-start
  117.2 0.0 copy-done
  117.2 0.5 convolution_bitcast_fusion.1
  117.7 65.6 %all_gather.20 = f32[16,4096]{1,0:T(8,128)S(1)} all-gather(f32[16,128]{1,0:T(8,128)S(1)} %convolution_bitcast_fusion.1), channel_id=1, replica_groups=mesh['grp'=8,'mem'=4] {'grp','mem'}, dimensions={1}, use_global_device_ids=true | all-gather | bytes 270336 | tf_op jit(solution)/shard_map/all_gather | solution.py:35
  183.3 15.9 %fusion.68 = f32[4096,1024]{1,0:T(8,128)} fusion(f32[16,4096]{1,0:T(8,128)S(1)} %all_gather.20, f32[16,1024]{1,0:T(8,128)S(1)} %copy-done), kind=kOutput, calls=%fused_computation.75 | convolution fusion | flops 805306368 | bytes 17104896 | tf_op jit(solution)/shard_map/dot_general | solution.py:46
  199.3 0.3 reduce-window.24
  199.5 0.1 slice.24
  199.6 0.1 slice_reduce_fusion
  199.8 0.1 add_bitcast_fusion
  199.8 0.5 convolution_bitcast_fusion
  201.0 67.7 %all_gather.23 = f32[16,4096]{1,0:T(8,128)S(1)} all-gather(f32[16,128]{1,0:T(8,128)S(1)} %convolution_bitcast_fusion), channel_id=1, replica_groups=mesh['grp'=8,'mem'=4] {'grp','mem'}, dimensions={1}, use_global_device_ids=true | all-gather | bytes 270336 | tf_op jit(solution)/shard_map/all_gather | solution.py:35
  268.7 0.0 all-reduce.3.cloned.1.call-done
  268.7 1.7 fusion.25
  270.5 1.2 fusion.41
  271.6 0.0 copy-done.1
  271.6 14.8 %fusion.29 = f32[16,1024]{1,0:T(8,128)S(1)} fusion(f32[16,1024]{1,0:T(8,128)S(1)} %copy-done.1, f32[16,4096]{1,0:T(8,128)} %all-reduce.3.cloned.1.call-done, f32[4096,1024]{1,0:T(8,128)} %fusion.68, f32[4096]{0:T(1024)S(1)} %multiply_reduce_fusion.1, f32[1024]{0:T(1024)S(1)} %multiply_reduce_fusion.2, f32[16,1024]{1,0:T(8,128)S(1)} %fusion.41), kind=kOutput, calls=%fused_computation.28 | convolution fusion | flops 822132736 | bytes 17256448 | tf_op jit(solution)/shard_map/dot_general | solution.py:50
  286.4 0.5 fusion.49
  286.9 65.5 %all_gather.21 = f32[16,4096]{1,0:T(8,128)S(1)} all-gather(f32[16,128]{1,0:T(8,128)S(1)} %fusion.49), channel_id=1, replica_groups=mesh['grp'=8,'mem'=4] {'grp','mem'}, dimensions={1}, use_global_device_ids=true | all-gather | bytes 270336 | tf_op jit(solution)/shard_map/all_gather | solution.py:34
  352.4 0.0 copy-start.2
  352.4 17.2 %fusion.8 = f32[16,1024]{1,0:T(8,128)S(1)} fusion(f32[16,4096]{1,0:T(8,128)S(1)} %all_gather.21, f32[1,1024,4096]{2,1,0:T(8,128)} %param.11), kind=kOutput, calls=%fused_computation.8 | convolution fusion | flops 805306368 | bytes 17104896 | tf_op jit(solution)/shard_map/dot_general | solution.py:38
  369.6 14.3 %all_gather.22 = f32[16,4096]{1,0:T(8,128)S(1)} all-gather(f32[16,1024]{1,0:T(8,128)S(1)} %fusion.8), channel_id=1, replica_groups=mesh['grp'=8,'mem'=4] {'mem'}, dimensions={1}, use_global_device_ids=true | all-gather | bytes 327680 | tf_op jit(solution)/shard_map/all_gather | solution.py:43
  383.9 0.7 broadcast_select_fusion
  384.6 0.0 all-reduce.5.cloned.1.call-update
  384.6 15.9 %fusion.69 = f32[4096,1024]{1,0:T(8,128)} fusion(f32[16,4096]{1,0:T(8,128)S(1)} %all_gather.23, f32[16,1024]{1,0:T(8,128)S(1)} %copy-done), kind=kOutput, calls=%fused_computation.76 | convolution fusion | flops 805306368 | bytes 17104896 | tf_op jit(solution)/shard_map/dot_general | solution.py:46
  400.6 35.4 %all-reduce.5.cloned.1.call-done = f32[16,4096]{1,0:T(8,128)} async-done(((f32[16,4096]{1,0:T(8,128)}), f32[16,4096]{1,0:T(8,128)}) %all-reduce.5.cloned.1.call-update) | async-done | bytes 262160 | tf_op jit(solution)/shard_map/psum | solution.py:14
  436.0 1.7 fusion.24
  437.8 0.0 copy-done.2
  437.8 1.2 add_add_fusion
  439.0 15.4 %fusion.35 = f32[16,1024]{1,0:T(8,128)} fusion(f32[16,1024]{1,0:T(8,128)S(1)} %fusion.29, f32[16,4096]{1,0:T(8,128)} %all-reduce.5.cloned.1.call-done, f32[4096,1024]{1,0:T(8,128)} %fusion.69, f32[4096]{0:T(1024)S(1)} %multiply_reduce_fusion, f32[1024]{0:T(1024)S(1)} %multiply_reduce_fusion.2, f32[16,1024]{1,0:T(8,128)S(1)} %get-tuple-element.11), kind=kOutput, calls=%fused_computation.30 | convolution fusion | flops 822132736 | bytes 17256448 | tf_op jit(solution)/shard_map/dot_general | solution.py:50
  (6 shorter events, 0.2 us)
Async XLA Ops:
  7.2 110.0 %copy-start = (f32[16,1024]{1,0:T(8,128)S(1)}, f32[16,1024]{1,0:T(8,128)}, u32[]{:S(2)}) copy-start(f32[16,1024]{1,0:T(8,128)} %param.6) | copy-start | bytes 196612
  7.2 261.5 %all-reduce.3.cloned.1.call-start = ((), (), s32[]{:S(2)}) async-start(), calls=%async_computation | async-start | bytes 524288 | tf_op jit(solution)/shard_map/psum | solution.py:14
  101.4 170.2 %copy-start.1 = (f32[16,1024]{1,0:T(8,128)S(1)}, f32[16,1024]{1,0:T(8,128)}, u32[]{:S(2)}) copy-start(f32[16,1024]{1,0:T(8,128)} %param.7) | copy-start | bytes 196612
  117.1 318.9 %all-reduce.5.cloned.1.call-start = ((), (), s32[]{:S(2)}) async-start(), calls=%async_computation.1 | async-start | bytes 524288 | tf_op jit(solution)/shard_map/psum | solution.py:14
  352.4 85.3 %copy-start.2 = (f32[16,1024]{1,0:T(8,128)S(1)}, f32[16,1024]{1,0:T(8,128)}, u32[]{:S(2)}) copy-start(f32[16,1024]{1,0:T(8,128)} %param.8) | copy-start | bytes 196612
Sparse Core Ops, SparseCore 0:
  117.3 49.9 all-reduce.2
  384.7 51.2 all-reduce.4
where the time goes:
time: 462 us; the launch traced here: 461 us
  blocking collectives  299 us (65%)
  matrix products  105 us (23%)
  waiting for transfers between devices  35.5 us (8%)
  between operations  15.5 us (3%)
    all_gather x2, blocking collectives, body(): lax.all_gather(chosen_res, ('grp', 'mem'), axis=1, tiled=True)  137 us
    all_gather x2, blocking collectives, body(): lax.all_gather(chosen_pts, ('grp', 'mem'), axis=1, tiled=True)  133 us
    psum x2, waiting for transfers between devices, from_root(): return lax.psum(kept, axis)  35.4 us
    dot_general x2, matrix products, body(): lax.dot_general(block_res, matrix_rows, (((1,), (1,)), ((), ())), precisi...  34.3 us
    dot_general x2, matrix products, body(): lax.dot_general(points, block_pts, (((0,), (0,)), ((), ())), precision=hi...  31.8 us
    dot_general x2, matrix products, body(): lax.dot_general(assembled, kernel, (((1,), (1,)), ((), ())), precision=hi...  30.2 us
    all_gather x2, blocking collectives, body(): assembled = lax.all_gather(solved, 'mem', axis=1, tiled=True)  28.6 us
  transfers between devices with their start and end apart: 2, of which 1 were waited for; matrix products, arithmetic and copies ran while one was open for 7% of the time, Pallas kernels for 0%

commit v1 on v0

--- a/solution.py
+++ b/solution.py
@@ -1,3 +1,4 @@
+import functools
 import jax
 import jax.numpy as jnp
 from jax import lax
@@ -7,6 +8,21 @@
 STEPS = 2
 ridge_weight = 0.5
 kernel_scale = 0.125
+
+
+def get_the_ratios(array_here, named_axis):
+    w_next, f_now = (lax.axis_size(named_axis), lax.axis_index(named_axis))
+    prior, y2 = (array_here, 1)
+    while y2 < w_next:
+        wide_out = lax.ppermute(prior, named_axis, [(src_i, src_i ^ y2) for src_i in range(w_next)])
+        known = jnp.concatenate([prior, wide_out], 1)
+        long_array = jnp.concatenate([wide_out, prior], 1)
+        prior = jnp.where(f_now & y2 == 0, known, long_array)
+        y2 = 2 * y2
+    return prior
+
+
+manage_the_tasks = functools.partial(get_the_ratios, named_axis=("grp", "mem"))
 
 
 def from_root(value, axis, source):
@@ -31,7 +47,7 @@
         chosen_res = jnp.dot(residual, select, precision=highest)
         chosen_pts = jnp.dot(points, select, precision=highest)
         block_res, block_pts = (
-            lax.all_gather(chosen_res, ("grp", "mem"), axis=1, tiled=True),
+            manage_the_tasks(chosen_res),
             lax.all_gather(chosen_pts, ("grp", "mem"), axis=1, tiled=True),
         )
         matrix_rows = lax.dynamic_index_in_dim(inverse, block_id % slots, 0, keepdims=False)

time: 462 us -> 426 us (0.922); the launches traced: 461 us -> 417 us
  blocking collectives: 299 us -> 164 us
  waiting for transfers between devices: 35.5 us -> 90.9 us
  starting transfers between devices: 0.08 us -> 24.5 us
  matrix products: 105 us -> 116 us
    all_gather x2 -> x0, blocking collectives: 137 us -> none  [body(): lax.all_gather(chosen_res, ('grp', 'mem'), axis=1, tiled=True)]
    psum x2, waiting for transfers between devices: 35.4 us -> 74.3 us  [from_root(): return lax.psum(kept, axis)]
    ppermute x0 -> x10, waiting for transfers between devices: none -> 16.6 us  [get_the_ratios(): lax.ppermute(prior, named_axis, [(src_i, src_i ^ y2) for src_i in range(w...]
    ppermute x0 -> x10, starting transfers between devices: none -> 13.5 us  [get_the_ratios(): lax.ppermute(prior, named_axis, [(src_i, src_i ^ y2) for src_i in range(w...]
    psum x2, starting transfers between devices: 0.08 us -> 11 us  [from_root(): return lax.psum(kept, axis)]
    dot_general x2, matrix products: 30.2 us -> 39.4 us  [body(): lax.dot_general(assembled, kernel, (((1,), (1,)), ((), ())), precision=hi...]
  transfers between devices with their start and end apart: 2 -> 12, of which waited for: 1 -> 9; matrix products, arithmetic and copies ran while one was open for 7% -> 8% of each run, Pallas kernels for 0% -> 0%
where the time goes in v1:
time: 426 us; the launch traced here: 417 us
  blocking collectives  164 us (38%)
  matrix products  116 us (27%)
  waiting for transfers between devices  90.9 us (21%)
  starting transfers between devices  24.5 us (6%)
  between operations  15.9 us (4%)
  other arithmetic  4.35 us (1%)
    all_gather x2, blocking collectives, body(): lax.all_gather(chosen_pts, ('grp', 'mem'), axis=1, tiled=True)  135 us
    psum x2, waiting for transfers between devices, from_root(): return lax.psum(kept, axis)  74.3 us
    dot_general x2, matrix products, body(): lax.dot_general(assembled, kernel, (((1,), (1,)), ((), ())), precision=hi...  39.4 us
    dot_general x2, matrix products, body(): lax.dot_general(block_res, matrix_rows, (((1,), (1,)), ((), ())), precisi...  34.6 us
    dot_general x2, matrix products, body(): lax.dot_general(points, block_pts, (((0,), (0,)), ((), ())), precision=hi...  32.4 us
    all_gather x2, blocking collectives, body(): assembled = lax.all_gather(solved, 'mem', axis=1, tiled=True)  28.6 us
    ppermute x10, waiting for transfers between devices, get_the_ratios(): lax.ppermute(prior, named_axis, [(src_i, src_i ^ y2) for src_i in range(w...  16.6 us
    ppermute x10, starting transfers between devices, get_the_ratios(): lax.ppermute(prior, named_axis, [(src_i, src_i ^ y2) for src_i in range(w...  13.5 us
  transfers between devices with their start and end apart: 12, of which 9 were waited for; matrix products, arithmetic and copies ran while one was open for 8% of the time, Pallas kernels for 0%

profile of v1, /device:TPU:0, one launch (start us, length us, event | category | flops | bytes accessed | tf_op | source)
XLA Modules:
  0.0 417.1 jit_solution(17333382219469734317)
XLA Ops:
  7.2 0.0 copy-start
  7.2 0.0 all-reduce.3.cloned.1.call-start
  7.2 1.3 fusion.81
  8.5 2.0 convert_bitcast_fusion
  10.5 0.3 reduce-window.16
  10.8 0.1 slice.21
  10.9 0.1 slice_reduce_fusion.1
  11.0 0.1 add_bitcast_fusion.1
  11.1 1.4 convolution_bitcast_fusion.2
  12.4 3.1 collective-permute-start
  15.5 1.4 convolution_bitcast_fusion.1
  16.9 0.3 collective-permute-done
  17.2 3.0 collective-permute-start.1
  20.2 67.0 %all_gather.13 = f32[16,4096]{1,0:T(8,128)S(1)} all-gather(f32[16,128]{1,0:T(8,128)S(1)} %convolution_bitcast_fusion.1), channel_id=1, replica_groups=mesh['grp'=8,'mem'=4] {'grp','mem'}, dimensions={1}, use_global_device_ids=true | all-gather | bytes 270336 | tf_op jit(solution)/shard_map/all_gather | solution.py:51
  87.2 0.0 collective-permute-done.1
  87.2 0.0 copy-start.1
  87.3 0.1 collective-permute-start.2
  87.3 16.6 %fusion.82 = f32[4096,1024]{0,1:T(8,128)} fusion(f32[16,4096]{1,0:T(8,128)S(1)} %all_gather.13, f32[16,1024]{1,0:T(8,128)} %param.6), kind=kOutput, calls=%fused_computation.99 | convolution fusion | flops 805306368 | bytes 17104896 | tf_op jit(solution)/shard_map/dot_general | solution.py:62
  103.9 0.3 reduce-window.24
  104.2 0.1 slice.24
  104.3 0.0 collective-permute-done.2
  104.3 0.1 collective-permute-start.3
  104.4 0.1 slice_reduce_fusion
  104.5 4.4 %collective-permute-done.3 = f32[16,1024]{1,0:T(8,128)S(1)} collective-permute-done((f32[16,1024]{1,0:T(8,128)S(1)}, f32[16,1024]{1,0:T(8,128)S(1)}, u32[]{:S(2)}, u32[]{:S(2)}) %collective-permute-start.3) | collective-permute-done | bytes 65568 | tf_op jit(solution)/shard_map/ppermute | solution.py:17
  108.9 1.5 collective-permute-start.4
  110.4 0.1 add_bitcast_fusion
  111.1 0.0 copy-done
  111.1 2.9 collective-permute-done.4
  114.1 17.3 %fusion.10 = f32[16,1024]{1,0:T(8,128)S(1)} fusion(f32[1,1024,4096]{2,1,0:T(8,128)} %param.11, f32[16,2048]{1,0:T(8,128)S(1)} %collective-permute-done.4, f32[16,2048]{1,0:T(8,128)S(1)} %maximum_select_fusion.4, pred[]{:T(512)S(6)} %eq.44), kind=kOutput, calls=%fused_computation.10 | convolution fusion | flops 805502976 | bytes 17104896 | tf_op jit(solution)/shard_map/dot_general | solution.py:54
  131.3 14.0 %all_gather.12 = f32[16,4096]{1,0:T(8,128)S(1)} all-gather(f32[16,1024]{1,0:T(8,128)S(1)} %fusion.10), channel_id=1, replica_groups=mesh['grp'=8,'mem'=4] {'mem'}, dimensions={1}, use_global_device_ids=true | all-gather | bytes 327680 | tf_op jit(solution)/shard_map/all_gather | solution.py:59
  145.3 0.7 broadcast_select_fusion.1
  146.0 0.0 all-reduce.3.cloned.1.call-update
  146.0 11.0 %all-reduce.5.cloned.1.call-start = ((), (), s32[]{:S(2)}) async-start(), calls=%async_computation.1 | async-start | bytes 524288 | tf_op jit(solution)/shard_map/psum | solution.py:30
  157.1 40.1 %all-reduce.3.cloned.1.call-done = f32[16,4096]{1,0:T(8,128)} async-done(((f32[16,4096]{1,0:T(8,128)}), f32[16,4096]{1,0:T(8,128)}) %all-reduce.3.cloned.1.call-update) | async-done | bytes 262160 | tf_op jit(solution)/shard_map/psum | solution.py:30
  197.2 1.7 fusion.25
  198.9 1.2 fusion.41
  200.1 0.0 copy-done.1
  200.1 19.4 %fusion.29 = f32[16,1024]{1,0:T(8,128)S(1)} fusion(f32[16,1024]{1,0:T(8,128)S(1)} %copy-done.1, f32[16,4096]{1,0:T(8,128)} %all-reduce.3.cloned.1.call-done, f32[4096,1024]{0,1:T(8,128)} %fusion.82, f32[4096]{0:T(1024)S(1)} %multiply_reduce_fusion.1, f32[1024]{0:T(1024)S(1)} %multiply_reduce_fusion.2, f32[16,1024]{1,0:T(8,128)S(1)} %fusion.41), kind=kOutput, calls=%fused_computation.28 | convolution fusion | flops 822132736 | bytes 17256448 | tf_op jit(solution)/shard_map/dot_general | solution.py:66
  219.5 0.5 fusion.49
  220.1 1.6 collective-permute-start.5
  221.6 2.2 collective-permute-done.5
  223.8 2.4 collective-permute-start.6
  226.2 2.2 collective-permute-done.6
  228.4 0.0 collective-permute-start.7
  228.4 1.2 collective-permute-done.7
  229.6 0.9 collective-permute-start.8
  230.5 3.4 collective-permute-done.8
  234.0 0.9 collective-permute-start.9
  234.9 0.5 convolution_bitcast_fusion
  236.1 68.2 %all_gather.15 = f32[16,4096]{1,0:T(8,128)S(1)} all-gather(f32[16,128]{1,0:T(8,128)S(1)} %convolution_bitcast_fusion), channel_id=1, replica_groups=mesh['grp'=8,'mem'=4] {'grp','mem'}, dimensions={1}, use_global_device_ids=true | all-gather | bytes 270336 | tf_op jit(solution)/shard_map/all_gather | solution.py:51
  304.2 0.0 copy-start.2
  304.2 0.0 collective-permute-done.9
  304.2 17.3 %fusion.8 = f32[16,1024]{1,0:T(8,128)S(1)} fusion(f32[1,1024,4096]{2,1,0:T(8,128)} %param.11, f32[16,2048]{1,0:T(8,128)S(1)} %collective-permute-done.9, f32[16,2048]{1,0:T(8,128)S(1)} %maximum_select_fusion.5, pred[]{:T(512)S(6)} %eq.44), kind=kOutput, calls=%fused_computation.8 | convolution fusion | flops 805502976 | bytes 17104896 | tf_op jit(solution)/shard_map/dot_general | solution.py:54
  321.5 14.6 %all_gather.14 = f32[16,4096]{1,0:T(8,128)S(1)} all-gather(f32[16,1024]{1,0:T(8,128)S(1)} %fusion.8), channel_id=1, replica_groups=mesh['grp'=8,'mem'=4] {'mem'}, dimensions={1}, use_global_device_ids=true | all-gather | bytes 327680 | tf_op jit(solution)/shard_map/all_gather | solution.py:59
  336.1 0.7 broadcast_select_fusion
  336.8 0.0 all-reduce.5.cloned.1.call-update
  336.8 15.8 %fusion.83 = f32[4096,1024]{0,1:T(8,128)} fusion(f32[16,4096]{1,0:T(8,128)S(1)} %all_gather.15, f32[16,1024]{1,0:T(8,128)S(1)} %copy-done), kind=kOutput, calls=%fused_computation.100 | convolution fusion | flops 805306368 | bytes 17104896 | tf_op jit(solution)/shard_map/dot_general | solution.py:62
  352.7 34.2 %all-reduce.5.cloned.1.call-done = f32[16,4096]{1,0:T(8,128)} async-done(((f32[16,4096]{1,0:T(8,128)}), f32[16,4096]{1,0:T(8,128)}) %all-reduce.5.cloned.1.call-update) | async-done | bytes 262160 | tf_op jit(solution)/shard_map/psum | solution.py:30
  386.9 1.7 fusion.24
  388.7 0.0 copy-done.2
  388.7 1.2 add_add_fusion
  389.9 20.0 %fusion.35 = f32[16,1024]{1,0:T(8,128)} fusion(f32[16,1024]{1,0:T(8,128)S(1)} %fusion.29, f32[16,4096]{1,0:T(8,128)} %all-reduce.5.cloned.1.call-done, f32[4096,1024]{0,1:T(8,128)} %fusion.83, f32[4096]{0:T(1024)S(1)} %multiply_reduce_fusion, f32[1024]{0:T(1024)S(1)} %multiply_reduce_fusion.2, f32[16,1024]{1,0:T(8,128)S(1)} %get-tuple-element.11), kind=kOutput, calls=%fused_computation.30 | convolution fusion | flops 822132736 | bytes 17256448 | tf_op jit(solution)/shard_map/dot_general | solution.py:66
  (14 shorter events, 0.2 us)
Async XLA Ops:
  7.2 103.9 %copy-start = (f32[16,1024]{1,0:T(8,128)S(1)}, f32[16,1024]{1,0:T(8,128)}, u32[]{:S(2)}) copy-start(f32[16,1024]{1,0:T(8,128)} %param.6) | copy-start | bytes 196612
  7.2 190.0 %all-reduce.3.cloned.1.call-start = ((), (), s32[]{:S(2)}) async-start(), calls=%async_computation | async-start | bytes 524288 | tf_op jit(solution)/shard_map/psum | solution.py:30
  12.4 4.7 %collective-permute-start = (f32[16,128]{1,0:T(8,128)S(1)}, f32[16,128]{1,0:T(8,128)S(1)}, u32[]{:S(2)}, u32[]{:S(2)}) collective-permute-start(f32[16,128]{1,0:T(8,128)S(1)} %convolution_bitcast_fusion.2), channel_id=1, source_target_pairs={{0,1},{1,0},{2,3},{3,2},{4,5},{5,4},{6,7},{7,6},{8,9},{9,8},{10,11... | collective-permute-start | bytes 24584 | tf_op jit(solution)/shard_map/ppermute | solution.py:17
  17.2 70.1 %collective-permute-start.1 = (f32[16,256]{1,0:T(8,128)S(1)}, f32[16,256]{1,0:T(8,128)S(1)}, u32[]{:S(2)}, u32[]{:S(2)}) collective-permute-start(f32[16,256]{1,0:T(8,128)S(1)} %maximum_select_fusion.10), channel_id=1, source_target_pairs={{0,2},{1,3},{2,0},{3,1},{4,6},{5,7},{6,4},{7,5},{8,10},{9,11},{10,... | collective-permute-start | bytes 49160 | tf_op jit(solution)/shard_map/ppermute | solution.py:17
  87.2 112.8 %copy-start.1 = (f32[16,1024]{1,0:T(8,128)S(1)}, f32[16,1024]{1,0:T(8,128)}, u32[]{:S(2)}) copy-start(f32[16,1024]{1,0:T(8,128)} %param.7) | copy-start | bytes 196612
  87.3 17.0 %collective-permute-start.2 = (f32[16,512]{1,0:T(8,128)S(1)}, f32[16,512]{1,0:T(8,128)S(1)}, u32[]{:S(2)}, u32[]{:S(2)}) collective-permute-start(f32[16,512]{1,0:T(8,128)S(1)} %maximum_select_fusion.8), channel_id=1, source_target_pairs={{0,4},{1,5},{2,6},{3,7},{4,0},{5,1},{6,2},{7,3},{8,12},{9,13},{10,... | collective-permute-start | bytes 98312 | tf_op jit(solution)/shard_map/ppermute | solution.py:17
  104.3 4.6 %collective-permute-start.3 = (f32[16,1024]{1,0:T(8,128)S(1)}, f32[16,1024]{1,0:T(8,128)S(1)}, u32[]{:S(2)}, u32[]{:S(2)}) collective-permute-start(f32[16,1024]{1,0:T(8,128)S(1)} %maximum_select_fusion.6), channel_id=1, source_target_pairs={{0,8},{1,9},{2,10},{3,11},{4,12},{5,13},{6,14},{7,15},{8,0},{9,1},... | collective-permute-start | bytes 196616 | tf_op jit(solution)/shard_map/ppermute | solution.py:17
  108.9 5.2 %collective-permute-start.4 = (f32[16,2048]{1,0:T(8,128)S(1)}, f32[16,2048]{1,0:T(8,128)S(1)}, u32[]{:S(2)}, u32[]{:S(2)}) collective-permute-start(f32[16,2048]{1,0:T(8,128)S(1)} %maximum_select_fusion.4), channel_id=1, source_target_pairs={{0,16},{1,17},{2,18},{3,19},{4,20},{5,21},{6,22},{7,23},{8,24},{9,... | collective-permute-start | bytes 393224 | tf_op jit(solution)/shard_map/ppermute | solution.py:17
  146.0 240.9 %all-reduce.5.cloned.1.call-start = ((), (), s32[]{:S(2)}) async-start(), calls=%async_computation.1 | async-start | bytes 524288 | tf_op jit(solution)/shard_map/psum | solution.py:30
  220.1 3.7 collective-permute-start.5
  223.8 4.6 %collective-permute-start.6 = (f32[16,256]{1,0:T(8,128)S(1)}, f32[16,256]{1,0:T(8,128)S(1)}, u32[]{:S(2)}, u32[]{:S(2)}) collective-permute-start(f32[16,256]{1,0:T(8,128)S(1)} %maximum_select_fusion.11), channel_id=1, source_target_pairs={{0,2},{1,3},{2,0},{3,1},{4,6},{5,7},{6,4},{7,5},{8,10},{9,11},{10,... | collective-permute-start | bytes 49160 | tf_op jit(solution)/shard_map/ppermute | solution.py:17
  228.4 1.2 collective-permute-start.7
  229.6 4.3 %collective-permute-start.8 = (f32[16,1024]{1,0:T(8,128)S(1)}, f32[16,1024]{1,0:T(8,128)S(1)}, u32[]{:S(2)}, u32[]{:S(2)}) collective-permute-start(f32[16,1024]{1,0:T(8,128)S(1)} %maximum_select_fusion.7), channel_id=1, source_target_pairs={{0,8},{1,9},{2,10},{3,11},{4,12},{5,13},{6,14},{7,15},{8,0},{9,1},... | collective-permute-start | bytes 196616 | tf_op jit(solution)/shard_map/ppermute | solution.py:17
  234.0 70.2 %collective-permute-start.9 = (f32[16,2048]{1,0:T(8,128)S(1)}, f32[16,2048]{1,0:T(8,128)S(1)}, u32[]{:S(2)}, u32[]{:S(2)}) collective-permute-start(f32[16,2048]{1,0:T(8,128)S(1)} %maximum_select_fusion.5), channel_id=1, source_target_pairs={{0,16},{1,17},{2,18},{3,19},{4,20},{5,21},{6,22},{7,23},{8,24},{9,... | collective-permute-start | bytes 393224 | tf_op jit(solution)/shard_map/ppermute | solution.py:17
  304.2 84.5 %copy-start.2 = (f32[16,1024]{1,0:T(8,128)S(1)}, f32[16,1024]{1,0:T(8,128)}, u32[]{:S(2)}) copy-start(f32[16,1024]{1,0:T(8,128)} %param.8) | copy-start | bytes 196612
Sparse Core Ops, SparseCore 0:
  146.2 50.9 all-reduce.2
  337.0 49.9 all-reduce.4
